TPU v7x, 32 devices: a whole 2x2x4 slice. The times are simulated.
32 devices in a mesh: occ: 4 (over z), vir: 8 (over y, x, core).
Axes of the slice: x: 2, y: 2, z: 4, core: 2. Of those that a mesh axis runs over, the one named last changes fastest.
Arguments:
- lam: bfloat16 [4096, 12288], P('occ', 'vir'), may hold values from -6 to 6
- integrals: bfloat16 [12288, 1024], P('vir', 'occ'), may hold values from -0.21875 to 0.21875
- occ_sym: int32 [32], P('occ'), may hold values from 0 to 7, as said below
- cd_sym: int32 [96], P('vir'), may hold values from 0 to 7
- ab_sym: int32 [8], replicated, may hold values from 0 to 7
Outputs:
- ladder: bfloat16 [4096, 1024], P('occ', 'vir')
Inputs may be any that keep to these rules, and one draw needn't show every extreme that they name: `occ_sym`: in each aligned block of 8 tiles (those of one index of occ) each representation labels the same number of tiles, 1 of them.
All inputs are finite; a program needn't handle non-finite values.
Results may differ from a plain program's by a relative error of at most 0.001.
Values may be sent and summed in bfloat16 or wider, within the bound.
No kernel may reach another device: no remote copies, remote signals or barrier semaphores. Data moves between devices by JAX's collectives and lax.ppermute only.
A program may use at most 128 MiB of HBM per device.

v0:
```python
import jax
import jax.numpy as jnp
from jax import lax
from jax.sharding import PartitionSpec as P


def on_device(lam, integrals, occ_sym, cd_sym, ab_sym):
    row_tiles = occ_sym.shape[0]
    cd_tiles = cd_sym.shape[0]
    tile_edge = lam.shape[0] // row_tiles
    lam_mask = (occ_sym[:, None] == cd_sym[None, :]).astype(jnp.bfloat16)
    lam_kept = (
        lam.reshape(row_tiles, tile_edge, cd_tiles, tile_edge) * lam_mask[:, None, :, None]
    ).reshape(lam.shape)
    own_cols = integrals.shape[1] // tile_edge
    own_sym = lax.dynamic_slice_in_dim(ab_sym, lax.axis_index("occ") * own_cols, own_cols)
    int_mask = (cd_sym[:, None] == own_sym[None, :]).astype(jnp.bfloat16)
    int_kept = (
        integrals.reshape(cd_tiles, tile_edge, own_cols, tile_edge) * int_mask[:, None, :, None]
    ).reshape(integrals.shape)
    partial_sum = jnp.dot(
        lam_kept,
        lax.all_gather(int_kept, "occ", axis=1, tiled=True),
        preferred_element_type=jnp.float32,
    )
    summed = lax.psum_scatter(partial_sum, "vir", scatter_dimension=1, tiled=True)
    return summed.astype(jnp.bfloat16)


def solution(mesh):
    in_specs = (P("occ", "vir"), P("vir", "occ"), P("occ"), P("vir"), P())
    out_specs = P("occ", "vir")
    return jax.shard_map(
        on_device, mesh=mesh, in_specs=in_specs, out_specs=out_specs, check_vma=False
    )
```

profile of v0, /device:TPU:0, one launch (start us, length us, event | category | flops | bytes accessed | tf_op | source)
XLA Modules:
  0.0 143.1 jit_solution(13634556950871698784)
XLA Ops:
  6.5 0.0 copy-start
  6.5 0.0 all-gather.2.cloned.1.call-start
  6.5 0.9 dynamic_slice.3
  7.4 0.8 compare_convert_fusion
  8.2 0.5 mul.29
  8.7 2.1 %bitcast_multiply_fusion.2 = bf16[1536,256]{1,0:T(8,128)(2,1)} fusion(bf16[1536,256]{1,0:T(8,128)(2,1)} %param.6, bf16[192,8,2,128]{3,2,1,0:T(2,128)(2,1)S(1)} %bitcast.13), kind=kLoop, calls=%fused_computation.3 | loop fusion | flops 393216 | bytes 2359296 | tf_op jit(solution)/shard_map/mul | solution.py:19
  10.9 0.0 all-gather.2.cloned.1.call-update
  10.9 0.0 copy-start.2
  10.9 0.0 copy-start.3
  10.9 0.0 reduce-scatter.2.cloned.1.call-start
  11.0 0.0 copy-done
  11.0 2.9 %copy.6 = bf16[1024,1536]{0,1:T(8,128)(2,1)} copy(bf16[1024,1536]{1,0:T(8,128)(2,1)S(1)} %copy-done) | data formatting | bytes 6291456 | tf_op args[0]
  13.8 0.0 copy-done.2
  13.8 0.0 copy-done.3
  13.9 0.0 copy-start.1
  13.9 0.1 compare_convert_fusion.1
  13.9 63.2 %all-gather.2.cloned.1.call-done = bf16[1536,1024]{1,0:T(8,128)(2,1)} async-done(((bf16[1536,256]{1,0:T(8,128)(2,1)}), bf16[1536,1024]{1,0:T(8,128)(2,1)}) %all-gather.2.cloned.1.call-update) | async-done | bytes 3145744 | tf_op jit(solution)/shard_map/all_gather | solution.py:23
  77.2 0.5 mul.25
  77.6 0.0 copy-done.1
  77.6 7.1 %fusion = f32[1024,1024]{1,0:T(8,128)} fusion(bf16[1536,1024]{1,0:T(8,128)(2,1)} %all-gather.2.cloned.1.call-done, bf16[1024,1536]{0,1:T(8,128)(2,1)S(1)} %copy-done.1, bf16[192,8,8,128]{3,2,1,0:T(8,128)(2,1)S(1)} %bitcast.12), kind=kOutput, calls=%fused_computation.1 | convolution fusion | flops 3222798336 | bytes 13631488 | tf_op jit(solution)/shard_map/dot_general | solution.py:21
  84.8 0.0 reduce-scatter.2.cloned.1.call-update
  84.8 49.7 %reduce-scatter.2.cloned.1.call-done = f32[1024,128]{1,0:T(8,128)} async-done(((f32[1024,1024]{1,0:T(8,128)}), f32[1024,128]{1,0:T(8,128)}) %reduce-scatter.2.cloned.1.call-update) | async-done | bytes 524304 | tf_op jit(solution)/shard_map/reduce_scatter | solution.py:26
  134.5 1.8 %convert_element_type.19 = bf16[1024,128]{1,0:T(8,128)(2,1)} convert(f32[1024,128]{1,0:T(8,128)} %reduce-scatter.2.cloned.1.call-done) | non-fusion elementwise | flops 131072 | bytes 786432 | tf_op jit(solution)/shard_map/convert_element_type | solution.py:27
Async XLA Ops:
  6.5 4.4 %copy-start = (bf16[1024,1536]{1,0:T(8,128)(2,1)S(1)}, bf16[1024,1536]{1,0:T(8,128)(2,1)}, u32[]{:S(2)}) copy-start(bf16[1024,1536]{1,0:T(8,128)(2,1)} %param.5) | copy-start | bytes 9437188
  6.5 70.6 %all-gather.2.cloned.1.call-start = ((), (), s32[]{:S(2)}) async-start(), calls=%async_computation.1 | async-start | bytes 3932160 | tf_op jit(solution)/shard_map/all_gather | solution.py:23
  10.9 3.0 %copy-start.2 = (s32[12]{0:T(128)S(1)}, s32[12]{0:T(128)}, u32[]{:S(2)}) copy-start(s32[12]{0:T(128)} %param.8) | copy-start | bytes 148
  10.9 3.0 %copy-start.3 = (s32[8]{0:T(128)S(1)}, s32[8]{0:T(128)}, u32[]{:S(2)}) copy-start(s32[8]{0:T(128)} %param.7) | copy-start | bytes 100
  10.9 123.6 %reduce-scatter.2.cloned.1.call-start = ((), (), s32[]{:S(2)}) async-start(), calls=%async_computation.2 | async-start | bytes 4718592 | tf_op jit(solution)/shard_map/reduce_scatter | solution.py:26
  13.9 63.8 %copy-start.1 = (bf16[1024,1536]{0,1:T(8,128)(2,1)S(1)}, bf16[1024,1536]{0,1:T(8,128)(2,1)}, u32[]{:S(2)}) copy-start(bf16[1024,1536]{0,1:T(8,128)(2,1)} %copy.6) | copy-start | bytes 9437188
Sparse Core Ops, SparseCore 0:
  11.0 66.1 all-gather.1
  84.9 49.4 reduce-scatter.1
where the time goes:
time: 143 us
  waiting for transfers between devices  113 us (79%)
  between operations  13.5 us (9%)
  matrix products  7.13 us (5%)
  other arithmetic  4.79 us (3%)
  local copies, waits for them, and re-layouts  4.73 us (3%)
    all_gather x1, waiting for transfers between devices, on_device(): lax.all_gather(int_kept, 'occ', axis=1, tiled=True)  63.2 us
    reduce_scatter x1, waiting for transfers between devices, on_device(): lax.psum_scatter(partial_sum, 'vir', scatter_dimension=1, tiled=True)  49.7 us
    dot_general x1, matrix products, on_device(): jnp.dot(lam_kept, lax.all_gather(int_kept, 'occ', axis=1, tiled=True), pr...  7.13 us
    unnamed x9, local copies, waits for them, and re-layouts  2.9 us
  transfers between devices with their start and end apart: 2, of which 2 were waited for; matrix products, arithmetic and copies ran while one was open for 2% of the time, Pallas kernels for 0%

commit v1 on v0

v1 whole, which is shorter than its diff:
```python
import jax
import jax.numpy as jnp
from jax import lax
from jax.sharding import PartitionSpec as P


def on_device(lam, integrals, occ_sym, cd_sym, ab_sym):
    row_tiles = occ_sym.shape[0]
    cd_tiles = cd_sym.shape[0]
    tile_edge = lam.shape[0] // row_tiles
    col_tiles = ab_sym.shape[0]
    own_cols = integrals.shape[1] // tile_edge
    row_of = jnp.argmax(occ_sym[None, :] == ab_sym[:, None], axis=1)
    own_sym = lax.dynamic_slice_in_dim(ab_sym, lax.axis_index("occ") * own_cols, own_cols)
    int_mask = (cd_sym[:, None] == own_sym[None, :]).astype(jnp.bfloat16)
    int_kept = (
        integrals.reshape(cd_tiles, tile_edge, own_cols, tile_edge) * int_mask[:, None, :, None]
    ).reshape(integrals.shape)
    int_all = lax.all_gather(int_kept, "occ", axis=1, tiled=True)
    int_cols = int_all.reshape(cd_tiles * tile_edge, col_tiles, tile_edge)
    lam_rows = lam.reshape(row_tiles, tile_edge, cd_tiles * tile_edge)[row_of]
    partial_sum = jnp.einsum(
        "trk,ktc->rtc", lam_rows, int_cols, preferred_element_type=jnp.float32
    ).reshape(tile_edge, col_tiles * tile_edge)
    summed = lax.psum_scatter(partial_sum, "vir", scatter_dimension=1, tiled=True)
    own_row = row_of[lax.axis_index("vir")]
    keep = (jnp.arange(row_tiles) == own_row)[:, None, None]
    out = jnp.where(keep, summed.astype(jnp.bfloat16)[None], jnp.zeros((), jnp.bfloat16))
    return out.reshape(row_tiles * tile_edge, summed.shape[1])


def solution(mesh):
    in_specs = (P("occ", "vir"), P("vir", "occ"), P("occ"), P("vir"), P())
    out_specs = P("occ", "vir")
    return jax.shard_map(
        on_device, mesh=mesh, in_specs=in_specs, out_specs=out_specs, check_vma=False
    )
```

time: 143 us -> 128 us (0.90)
  waiting for transfers between devices: 113 us -> 94.3 us
  local copies, waits for them, and re-layouts: 4.73 us -> 9.28 us
  matrix products: 7.13 us -> 4.61 us
    reduce_scatter x1, waiting for transfers between devices: 49.7 us -> 31.2 us  [on_device(): lax.psum_scatter(partial_sum, 'vir', scatter_dimension=1, tiled=True)]
    all_gather x0 -> x1, local copies, waits for them, and re-layouts: none -> 4.73 us  [on_device(): int_all = lax.all_gather(int_kept, 'occ', axis=1, tiled=True)]
    unnamed x9 -> x6, local copies, waits for them, and re-layouts: 2.9 us -> 0.01 us
    dot_general x1, matrix products: 7.13 us -> 4.61 us  [on_device(): jnp.einsum('trk,ktc->rtc', lam_rows, int_cols, preferred_element_type=jnp...]
    gather x0 -> x1, local copies, waits for them, and re-layouts: none -> 2.41 us  [on_device(): lam_rows = lam.reshape(row_tiles, tile_edge, cd_tiles * tile_edge)[row_of]]
  transfers between devices with their start and end apart: 2 -> 2, of which waited for: 2 -> 2; matrix products, arithmetic and copies ran while one was open for 2% -> 3% of each run, Pallas kernels for 0% -> 0%
where the time goes in v1:
time: 128 us
  waiting for transfers between devices  94.3 us (74%)
  between operations  13.5 us (11%)
  local copies, waits for them, and re-layouts  9.28 us (7%)
  other arithmetic  6.1 us (5%)
  matrix products  4.61 us (4%)
    all_gather x1, waiting for transfers between devices, on_device(): int_all = lax.all_gather(int_kept, 'occ', axis=1, tiled=True)  63.1 us
    reduce_scatter x1, waiting for transfers between devices, on_device(): lax.psum_scatter(partial_sum, 'vir', scatter_dimension=1, tiled=True)  31.2 us
    all_gather x1, local copies, waits for them, and re-layouts, on_device(): int_all = lax.all_gather(int_kept, 'occ', axis=1, tiled=True)  4.73 us
    dot_general x1, matrix products, on_device(): jnp.einsum('trk,ktc->rtc', lam_rows, int_cols, preferred_element_type=jnp...  4.61 us
  transfers between devices with their start and end apart: 2, of which 2 were waited for; matrix products, arithmetic and copies ran while one was open for 3% of the time, Pallas kernels for 0%

profile of v1, /device:TPU:0, one launch (start us, length us, event | category | flops | bytes accessed | tf_op | source)
XLA Modules:
  0.0 127.8 jit_solution(6832166300648707751)
XLA Ops:
  6.5 0.0 copy-start
  6.5 0.0 all-gather.2.cloned.1.call-start
  6.6 0.9 dynamic_slice.7
  7.4 0.8 compare_convert_fusion
  8.3 0.5 mul.15
  8.7 2.2 %bitcast_multiply_fusion = bf16[1536,256]{1,0:T(8,128)(2,1)} fusion(bf16[1536,256]{1,0:T(8,128)(2,1)} %param.6, bf16[192,8,2,128]{3,2,1,0:T(2,128)(2,1)S(1)} %bitcast.18), kind=kLoop, calls=%fused_computation.1 | loop fusion | flops 393216 | bytes 2359296 | tf_op jit(solution)/shard_map/mul | solution.py:17
  10.9 0.0 all-gather.2.cloned.1.call-update
  10.9 0.0 reduce-scatter.2.cloned.1.call-start
  11.0 0.0 copy-done.2
  11.0 0.0 copy-done.1
  11.0 0.7 iota_reduce_fusion
  11.7 0.0 copy-done
  11.7 2.4 %gather_fusion = bf16[8,128,1536]{2,1,0:T(8,128)(2,1)} fusion(bf16[8,128,1536]{2,1,0:T(8,128)(2,1)S(1)} %bitcast.16, s32[1024]{0:T(1024)S(1)} %pad_clamp_fusion), kind=kCustom, calls=%fused_computation | custom fusion | bytes 6291488 | tf_op jit(solution)/shard_map/gather | solution.py:21
  14.1 63.1 %all-gather.2.cloned.1.call-done = bf16[1536,1024]{1,0:T(8,128)(2,1)} async-done(((bf16[1536,256]{1,0:T(8,128)(2,1)}), bf16[1536,1024]{1,0:T(8,128)(2,1)}) %all-gather.2.cloned.1.call-update) | async-done | bytes 3145744 | tf_op jit(solution)/shard_map/all_gather | solution.py:19
  77.2 4.7 %copy.8 = bf16[1536,1024]{0,1:T(8,128)(2,1)} copy(bf16[1536,1024]{1,0:T(8,128)(2,1)} %all-gather.2.cloned.1.call-done) | data formatting | bytes 6291456 | tf_op jit(solution)/shard_map/all_gather | solution.py:19
  81.9 4.6 %fusion = f32[8,128,128]{2,1,0:T(8,128)} fusion(bf16[1536,8,128]{0,2,1:T(8,128)(2,1)} %bitcast.17, bf16[8,128,1536]{2,1,0:T(8,128)(2,1)} %gather_fusion), kind=kOutput, calls=%fused_computation.9 | convolution fusion | flops 402653184 | bytes 6815744 | tf_op jit(solution)/shard_map/trk,ktc->rtc/dot_general | solution.py:22
  86.5 0.0 reduce-scatter.2.cloned.1.call-update
  86.6 0.6 dynamic_slice.6
  87.2 0.6 iota_compare_fusion
  87.8 0.1 broadcast_bitcast_fusion
  87.9 31.2 %reduce-scatter.2.cloned.1.call-done = f32[128,128]{0,1:T(8,128)} async-done(((f32[128,1024]{0,1:T(8,128)}), f32[128,128]{0,1:T(8,128)}) %reduce-scatter.2.cloned.1.call-update) | async-done | bytes 65552 | tf_op jit(solution)/shard_map/reduce_scatter | solution.py:25
  119.0 0.8 convert_element_type.11
  119.9 0.1 copy.9
  120.0 0.9 bitcast_select_fusion
  (4 shorter events, 0.0 us)
Async XLA Ops:
  6.5 5.2 %copy-start = (bf16[1024,1536]{1,0:T(8,128)(2,1)S(1)}, bf16[1024,1536]{1,0:T(8,128)(2,1)}, u32[]{:S(2)}) copy-start(bf16[1024,1536]{1,0:T(8,128)(2,1)} %param.5) | copy-start | bytes 9437188
  6.5 4.4 %copy-start.2 = (s32[8]{0:T(128)S(1)}, s32[8]{0:T(128)}, u32[]{:S(2)}) copy-start(s32[8]{0:T(128)} %param.9) | copy-start | bytes 100
  6.5 4.4 %copy-start.1 = (s32[8]{0:T(128)S(1)}, s32[8]{0:T(128)}, u32[]{:S(2)}) copy-start(s32[8]{0:T(128)} %param.7) | copy-start | bytes 100
  6.5 70.7 %all-gather.2.cloned.1.call-start = ((), (), s32[]{:S(2)}) async-start(), calls=%async_computation.1 | async-start | bytes 3932160 | tf_op jit(solution)/shard_map/all_gather | solution.py:19
  10.9 108.1 %reduce-scatter.2.cloned.1.call-start = ((), (), s32[]{:S(2)}) async-start(), calls=%async_computation.2 | async-start | bytes 589824 | tf_op jit(solution)/shard_map/reduce_scatter | solution.py:25
Sparse Core Ops, SparseCore 0:
  11.0 66.1 all-gather.1
  86.7 32.3 reduce-scatter.1

commit v2 on v1

--- a/solution.py
+++ b/solution.py
@@ -2,6 +2,21 @@
 import jax.numpy as jnp
 from jax import lax
 from jax.sharding import PartitionSpec as P
+
+
+def halving_reduce_scatter(parts, axis):
+    n = lax.axis_size(axis)
+    me = lax.axis_index(axis)
+    step = 1
+    while step < n:
+        bit = (me // step) % 2
+        pairs = parts.reshape(parts.shape[0] // 2, 2, *parts.shape[1:])
+        keep = lax.dynamic_index_in_dim(pairs, bit, axis=1, keepdims=False)
+        send = lax.dynamic_index_in_dim(pairs, 1 - bit, axis=1, keepdims=False)
+        perm = [(j, j ^ step) for j in range(n)]
+        parts = keep + lax.ppermute(send, axis, perm)
+        step *= 2
+    return parts[0]
 
 
 def on_device(lam, integrals, occ_sym, cd_sym, ab_sym):
@@ -20,9 +35,9 @@
     int_cols = int_all.reshape(cd_tiles * tile_edge, col_tiles, tile_edge)
     lam_rows = lam.reshape(row_tiles, tile_edge, cd_tiles * tile_edge)[row_of]
     partial_sum = jnp.einsum(
-        "trk,ktc->rtc", lam_rows, int_cols, preferred_element_type=jnp.float32
-    ).reshape(tile_edge, col_tiles * tile_edge)
-    summed = lax.psum_scatter(partial_sum, "vir", scatter_dimension=1, tiled=True)
+        "trk,ktc->trc", lam_rows, int_cols, preferred_element_type=jnp.float32
+    )
+    summed = halving_reduce_scatter(partial_sum, "vir")
     own_row = row_of[lax.axis_index("vir")]
     keep = (jnp.arange(row_tiles) == own_row)[:, None, None]
     out = jnp.where(keep, summed.astype(jnp.bfloat16)[None], jnp.zeros((), jnp.bfloat16))

time: 128 us -> 108 us (0.84)
  waiting for transfers between devices: 94.3 us -> 70.3 us
  starting transfers between devices: 0.04 us -> 3.14 us
    reduce_scatter x1 -> x0, waiting for transfers between devices: 31.2 us -> none  [on_device(): lax.psum_scatter(partial_sum, 'vir', scatter_dimension=1, tiled=True)]
    ppermute x0 -> x3, waiting for transfers between devices: none -> 7.27 us  [halving_reduce_scatter(): parts = keep + lax.ppermute(send, axis, perm)]
    ppermute x0 -> x3, starting transfers between devices: none -> 3.14 us  [halving_reduce_scatter(): parts = keep + lax.ppermute(send, axis, perm)]
    add x0 -> x2, other arithmetic: none -> 1.98 us  [halving_reduce_scatter(): parts = keep + lax.ppermute(send, axis, perm)]
  transfers between devices with their start and end apart: 2 -> 4, of which waited for: 2 -> 4; matrix products, arithmetic and copies ran while one was open for 3% -> 4% of each run, Pallas kernels for 0% -> 0%
where the time goes in v2:
time: 108 us
  waiting for transfers between devices  70.3 us (65%)
  between operations  13.6 us (13%)
  local copies, waits for them, and re-layouts  10 us (9%)
  other arithmetic  7.24 us (7%)
  matrix products  3.81 us (4%)
  starting transfers between devices  3.14 us (3%)
    all_gather x1, waiting for transfers between devices, on_device(): int_all = lax.all_gather(int_kept, 'occ', axis=1, tiled=True)  63.1 us
    ppermute x3, waiting for transfers between devices, halving_reduce_scatter(): parts = keep + lax.ppermute(send, axis, perm)  7.27 us
    all_gather x1, local copies, waits for them, and re-layouts, on_device(): int_all = lax.all_gather(int_kept, 'occ', axis=1, tiled=True)  4.73 us
    dot_general x1, matrix products, on_device(): jnp.einsum('trk,ktc->trc', lam_rows, int_cols, preferred_element_type=jnp...  3.81 us
    ppermute x3, starting transfers between devices, halving_reduce_scatter(): parts = keep + lax.ppermute(send, axis, perm)  3.14 us
    gather x1, local copies, waits for them, and re-layouts, on_device(): lam_rows = lam.reshape(row_tiles, tile_edge, cd_tiles * tile_edge)[row_of]  2.45 us
    mul x1, other arithmetic, on_device(): integrals.reshape(cd_tiles, tile_edge, own_cols, tile_edge)  2.16 us
  transfers between devices with their start and end apart: 4, of which 4 were waited for; matrix products, arithmetic and copies ran while one was open for 4% of the time, Pallas kernels for 0%

profile of v2, /device:TPU:0, one launch (start us, length us, event | category | flops | bytes accessed | tf_op | source)
XLA Modules:
  0.0 108.1 jit_solution(3838639812929130183)
XLA Ops:
  6.5 0.0 copy-start
  6.6 0.9 dynamic_slice.24
  7.4 0.8 compare_convert_fusion
  8.3 0.5 mul.15
  8.7 2.2 %bitcast_multiply_fusion = bf16[1536,256]{1,0:T(8,128)(2,1)} fusion(bf16[1536,256]{1,0:T(8,128)(2,1)} %param.6, bf16[192,8,2,128]{3,2,1,0:T(2,128)(2,1)S(1)} %bitcast.27), kind=kLoop, calls=%fused_computation.1 | loop fusion | flops 393216 | bytes 2359296 | tf_op jit(solution)/shard_map/mul | solution.py:32
  10.9 0.0 all-gather.2.cloned.1.call-update
  11.0 0.7 iota_reduce_fusion
  11.7 2.5 %gather_fusion = bf16[8,128,1536]{2,1,0:T(8,128)(2,1)} fusion(bf16[8,128,1536]{2,1,0:T(8,128)(2,1)S(1)} %bitcast.25, s32[1024]{0:T(1024)S(1)} %pad_clamp_fusion), kind=kCustom, calls=%fused_computation | custom fusion | bytes 6291488 | tf_op jit(solution)/shard_map/gather | solution.py:36
  14.1 63.1 %all-gather.2.cloned.1.call-done = bf16[1536,1024]{1,0:T(8,128)(2,1)} async-done(((bf16[1536,256]{1,0:T(8,128)(2,1)}), bf16[1536,1024]{1,0:T(8,128)(2,1)}) %all-gather.2.cloned.1.call-update) | async-done | bytes 3145744 | tf_op jit(solution)/shard_map/all_gather | solution.py:34
  77.2 4.7 %copy.10 = bf16[1536,1024]{0,1:T(8,128)(2,1)} copy(bf16[1536,1024]{1,0:T(8,128)(2,1)} %all-gather.2.cloned.1.call-done) | data formatting | bytes 6291456 | tf_op jit(solution)/shard_map/all_gather | solution.py:34
  81.9 3.8 %fusion.1 = f32[8,128,128]{2,1,0:T(8,128)S(1)} fusion(bf16[8,128,1536]{2,1,0:T(8,128)(2,1)} %gather_fusion, bf16[1536,8,128]{0,2,1:T(8,128)(2,1)} %bitcast.26), kind=kOutput, calls=%fused_computation.16 | convolution fusion | flops 402653184 | bytes 6815744 | tf_op jit(solution)/shard_map/trk,ktc->trc/dot_general | solution.py:37
  85.8 0.8 copy-done.1
  86.6 0.1 collective-permute-start
  86.7 1.6 %collective-permute-done = f32[4,128,128]{2,1,0:T(8,128)} collective-permute-done((f32[4,128,128]{2,1,0:T(8,128)S(1)}, f32[4,128,128]{2,1,0:T(8,128)}, u32[]{:S(2)}, u32[]{:S(2)}) %collective-permute-start) | collective-permute-done | bytes 262176 | tf_op jit(solution)/shard_map/ppermute | solution.py:17
  88.3 1.1 bitcast_add_fusion
  89.4 1.5 %collective-permute-start.1 = (f32[2,128,128]{2,1,0:T(8,128)S(1)}, f32[2,128,128]{2,1,0:T(8,128)}, u32[]{:S(2)}, u32[]{:S(2)}) collective-permute-start(f32[2,128,128]{2,1,0:T(8,128)S(1)} %dynamic-slice_bitcast_fusion.1), channel_id=1, source_target_pairs={{0,2},{1,3},{2,0},{3,1},{4,6},{5,7},{6,4},{7,5},{8,10},{9,11},{10,... | collective-permute-start | bytes 393224 | tf_op jit(solution)/shard_map/ppermute | solution.py:17
  90.9 0.6 dynamic_slice.23
  91.5 0.6 iota_compare_fusion
  92.2 2.9 %collective-permute-done.1 = f32[2,128,128]{2,1,0:T(8,128)} collective-permute-done((f32[2,128,128]{2,1,0:T(8,128)S(1)}, f32[2,128,128]{2,1,0:T(8,128)}, u32[]{:S(2)}, u32[]{:S(2)}) %collective-permute-start.1) | collective-permute-done | bytes 131104 | tf_op jit(solution)/shard_map/ppermute | solution.py:17
  95.1 0.9 bitcast_add_fusion.1
  96.0 1.5 %collective-permute-start.2 = (f32[1,128,128]{2,1,0:T(8,128)S(1)}, f32[1,128,128]{2,1,0:T(8,128)S(1)}, u32[]{:S(2)}, u32[]{:S(2)}) collective-permute-start(f32[1,128,128]{2,1,0:T(8,128)S(1)} %constant_dynamic-slice_fusion), channel_id=1, source_target_pairs={{0,4},{1,5},{2,6},{3,7},{4,0},{5,1},{6,2},{7,3},{8,12},{9,13},{10,... | collective-permute-start | bytes 196616 | tf_op jit(solution)/shard_map/ppermute | solution.py:17
  97.6 0.1 broadcast_bitcast_fusion
  97.6 2.7 %collective-permute-done.2 = f32[1,128,128]{2,1,0:T(8,128)S(1)} collective-permute-done((f32[1,128,128]{2,1,0:T(8,128)S(1)}, f32[1,128,128]{2,1,0:T(8,128)S(1)}, u32[]{:S(2)}, u32[]{:S(2)}) %collective-permute-start.2) | collective-permute-done | bytes 65568 | tf_op jit(solution)/shard_map/ppermute | solution.py:17
  100.4 0.9 bitcast_select_fusion
  (13 shorter events, 0.1 us)
Async XLA Ops:
  6.5 5.1 %copy-start = (bf16[1024,1536]{1,0:T(8,128)(2,1)S(1)}, bf16[1024,1536]{1,0:T(8,128)(2,1)}, u32[]{:S(2)}) copy-start(bf16[1024,1536]{1,0:T(8,128)(2,1)} %param.5) | copy-start | bytes 9437188
  6.5 4.4 %copy-start.3 = (s32[8]{0:T(128)S(1)}, s32[8]{0:T(128)}, u32[]{:S(2)}) copy-start(s32[8]{0:T(128)} %param.9) | copy-start | bytes 100
  6.5 4.4 %copy-start.2 = (s32[8]{0:T(128)S(1)}, s32[8]{0:T(128)}, u32[]{:S(2)}) copy-start(s32[8]{0:T(128)} %param.7) | copy-start | bytes 100
  6.5 70.7 %all-gather.2.cloned.1.call-start = ((), (), s32[]{:S(2)}) async-start(), calls=%async_computation | async-start | bytes 3932160 | tf_op jit(solution)/shard_map/all_gather | solution.py:34
  85.8 0.8 copy-start.1
  86.6 1.7 %collective-permute-start = (f32[4,128,128]{2,1,0:T(8,128)S(1)}, f32[4,128,128]{2,1,0:T(8,128)}, u32[]{:S(2)}, u32[]{:S(2)}) collective-permute-start(f32[4,128,128]{2,1,0:T(8,128)S(1)} %dynamic-slice_bitcast_fusion), channel_id=1, source_target_pairs={{0,1},{1,0},{2,3},{3,2},{4,5},{5,4},{6,7},{7,6},{8,9},{9,8},{10,11... | collective-permute-start | bytes 786440 | tf_op jit(solution)/shard_map/ppermute | solution.py:17
  89.4 5.7 %collective-permute-start.1 = (f32[2,128,128]{2,1,0:T(8,128)S(1)}, f32[2,128,128]{2,1,0:T(8,128)}, u32[]{:S(2)}, u32[]{:S(2)}) collective-permute-start(f32[2,128,128]{2,1,0:T(8,128)S(1)} %dynamic-slice_bitcast_fusion.1), channel_id=1, source_target_pairs={{0,2},{1,3},{2,0},{3,1},{4,6},{5,7},{6,4},{7,5},{8,10},{9,11},{10,... | collective-permute-start | bytes 393224 | tf_op jit(solution)/shard_map/ppermute | solution.py:17
  96.0 4.3 %collective-permute-start.2 = (f32[1,128,128]{2,1,0:T(8,128)S(1)}, f32[1,128,128]{2,1,0:T(8,128)S(1)}, u32[]{:S(2)}, u32[]{:S(2)}) collective-permute-start(f32[1,128,128]{2,1,0:T(8,128)S(1)} %constant_dynamic-slice_fusion), channel_id=1, source_target_pairs={{0,4},{1,5},{2,6},{3,7},{4,0},{5,1},{6,2},{7,3},{8,12},{9,13},{10,... | collective-permute-start | bytes 196616 | tf_op jit(solution)/shard_map/ppermute | solution.py:17
Sparse Core Ops, SparseCore 0:
  11.0 66.1 all-gather.1
